TPU v7x, 256 devices: a whole 4x4x8 slice. The times are simulated.
256 devices in a mesh: dom: 16 (over z, core), grp: 16 (over y, x).
Axes of the slice: x: 4, y: 4, z: 8, core: 2. Of those that a mesh axis runs over, the one named last changes fastest.
Arguments:
- positions: float32 [65536, 3, 128], P(('dom', 'grp')), may hold values from -4 to 4
- velocities: float32 [65536, 3, 128], P(('dom', 'grp')), may hold values from -9 to 9
- masses: float32 [65536, 128], P(('dom', 'grp')), may hold values from 0.3 to 3
- destination: int32 [65536], P(('dom', 'grp')), may hold values from 0 to 15, as said below
- group_ids: int32 [65536, 128], P(('dom', 'grp')), may hold values from 0 to 1023, as said below
- boundary_set: int32 [256, 64], P(('dom', 'grp')), may hold values from 0 to 511, as said below
- send_list: int32 [256, 16, 16], P(('dom', 'grp')), may hold values from 0 to 63, as said below
- send_count: int32 [256, 16], P(('dom', 'grp')), may hold values from 0 to 16, as said below
- partners: int32 [131072, 4], P(('dom', 'grp')), may hold values from 0 to 767, as said below
Outputs:
- energy: float32 [65536, 128], P(('dom', 'grp'))
- group_kinetic: float32 [1024], replicated
Inputs may be any that keep to these rules, and one draw needn't show every extreme that they name: Each block of 256 leaves sends at most 32 leaves to one destination; in each dom index one destination receives exactly 32 leaves from every block. `group_ids`: the particles of block b carry the 16 group numbers 4 * b to 4 * b + 15, taken modulo 1024, each at least once and no others. `boundary_set`: each row holds 64 distinct slot numbers. `send_list`: each row of 16 holds distinct positions. `send_count`: A block sends nothing to its own grp index; in each dom index one grp index receives 16 from every other block. `partners`: each row holds 4 distinct entry numbers of combined.
All inputs are finite; a program needn't handle non-finite values.
Results may differ from a plain program's by a relative error of at most 0.0003.
Values sent between devices are 32-bit elements; how exact they have to be, the bound alone decides.
No kernel may reach another device: no remote copies, remote signals or barrier semaphores. Data moves between devices by JAX's collectives and lax.ppermute only.
A program may use at most 64 MiB of HBM per device.

v0:
```python
import jax
import jax.numpy as jnp
from jax import lax
from jax.sharding import PartitionSpec as P

GSPAN = 16
GROUP_DEV = 4
softening = 0.0025
exact = lax.Precision.HIGHEST


def select_rows(table, index):
    count = table.shape[0]
    flat = table.reshape(count, -1)
    picker = (index.reshape(-1)[:, None] == jnp.arange(count, dtype=jnp.int32)[None, :]).astype(
        jnp.float32
    )
    chosen = jnp.dot(picker, flat, precision=exact, preferred_element_type=jnp.float32)
    return chosen.reshape(index.shape + table.shape[1:])


def tile_potential(targets, sources):
    distance = softening
    for component in range(3):
        offset = targets[:, None, component, :, None] - sources[:, :, component, None, :]
        distance = distance + offset * offset
    weights = sources[:, :, 3, None, :] * lax.rsqrt(distance)
    return -jnp.sum(weights, axis=(1, 3))


def slot_potential(owned, combined, pair_index, coupling):
    slot_count = owned.shape[0]
    leaf_width = owned.shape[2]
    block_rows = max(32, slot_count // 16)

    def one_block(inputs):
        targets, indices = inputs
        sources = select_rows(combined, indices)
        return tile_potential(targets, sources)

    result = lax.map(
        one_block,
        (
            owned.reshape(slot_count // block_rows, block_rows, 4, leaf_width),
            pair_index.reshape(slot_count // block_rows, block_rows, pair_index.shape[1]),
        ),
    )
    return result.reshape(slot_count, leaf_width) * coupling


def shards(
    positions,
    velocities,
    masses,
    destination,
    group_ids,
    boundary_set,
    send_list,
    send_count,
    partners,
):
    owners = lax.axis_size("grp")
    leaves = positions.shape[0]
    leaf_width = positions.shape[2]
    capacity = 2 * leaves // owners
    slot_count = owners * capacity
    groups = GROUP_DEV * lax.axis_size("dom") * owners
    block_index = lax.axis_index("dom") * owners + lax.axis_index("grp")
    first_group = block_index * GROUP_DEV
    mass_flat = masses.reshape(-1)
    group_flat = group_ids.reshape(-1)
    speeds = jnp.transpose(velocities, (1, 0, 2)).reshape(3, -1)
    local_ids = (group_flat - first_group) % groups
    member = (jnp.arange(GSPAN, dtype=jnp.int32)[:, None] == local_ids[None, :]).astype(jnp.float32)
    place = (
        (first_group + jnp.arange(GSPAN, dtype=jnp.int32))[:, None] % groups
        == jnp.arange(groups, dtype=jnp.int32)[None, :]
    ).astype(jnp.float32)

    def group_sums(stats):
        local_sums = jnp.einsum(
            "kp,gp->kg", stats, member, precision=exact, preferred_element_type=jnp.float32
        )
        return jnp.dot(local_sums, place, precision=exact, preferred_element_type=jnp.float32)

    first_sums = group_sums(
        jnp.concatenate([mass_flat[None, :], mass_flat[None, :] * speeds], axis=0)
    )
    mass_total, momentum = lax.psum((first_sums[0], first_sums[1:]), ("dom", "grp"))
    bulk_velocity = momentum / mass_total[None, :]
    bulk_local = jnp.einsum(
        "kq,gq->kg", bulk_velocity, place, precision=exact, preferred_element_type=jnp.float32
    )
    per_particle = jnp.dot(bulk_local, member, precision=exact, preferred_element_type=jnp.float32)
    relative = speeds - per_particle
    kinetic = 0.5 * jnp.sum(relative * relative, axis=0)
    heat_sum = lax.psum(group_sums((mass_flat * kinetic)[None, :])[0], ("dom", "grp"))
    group_kinetic = heat_sum / mass_total
    onehot = (destination[:, None] == jnp.arange(owners, dtype=jnp.int32)[None, :]).astype(
        jnp.int32
    )
    leaf_rank = jnp.sum((jnp.cumsum(onehot, axis=0) - onehot) * onehot, axis=1)
    target = destination * capacity + leaf_rank
    payload = jnp.concatenate([positions, masses[:, None, :]], axis=1)
    placing = (jnp.arange(slot_count, dtype=jnp.int32)[:, None] == target[None, :]).astype(
        jnp.float32
    )
    outgoing = jnp.dot(
        placing, payload.reshape(leaves, -1), precision=exact, preferred_element_type=jnp.float32
    ).reshape(slot_count, 4, leaf_width)
    owned = lax.all_to_all(outgoing, "grp", split_axis=0, concat_axis=0, tiled=True)
    set_size = boundary_set.shape[1]
    per_peer = send_list.shape[2]
    boundary = select_rows(owned, boundary_set[0])
    every_set = lax.all_gather(boundary, "grp", axis=0, tiled=True)
    all_lists, all_counts = (
        lax.all_gather(send_list, "grp", axis=0, tiled=True),
        lax.all_gather(send_count, "grp", axis=0, tiled=True),
    )
    my_index = lax.axis_index("grp")
    my_lists = jnp.take(all_lists, my_index, axis=1)
    my_counts = jnp.take(all_counts, my_index, axis=1)
    positions_in = jnp.arange(owners, dtype=jnp.int32)[:, None] * set_size + my_lists
    remote = select_rows(every_set, positions_in)
    is_live = jnp.arange(per_peer, dtype=jnp.int32)[None, :] < my_counts[:, None]
    remote = jnp.where(is_live[:, :, None, None], remote, jnp.zeros_like(remote))
    remote = remote.reshape(owners * per_peer, 4, leaf_width)
    combined = jnp.concatenate([owned, remote], axis=0)
    coupling = 1.0 / (partners.shape[1] * leaf_width)
    potential = slot_potential(owned, combined, partners, coupling)
    returned = lax.all_to_all(potential, "grp", split_axis=0, concat_axis=0, tiled=True)
    own_potential = jnp.einsum(
        "sl,sp->lp", placing, returned, precision=exact, preferred_element_type=jnp.float32
    )
    energy = kinetic.reshape(leaves, leaf_width) + own_potential
    return (energy, group_kinetic)


def solution(mesh):
    in_specs = (
        P(("dom", "grp"), None, None),
        P(("dom", "grp"), None, None),
        P(("dom", "grp"), None),
        P(("dom", "grp")),
        P(("dom", "grp"), None),
        P(("dom", "grp"), None),
        P(("dom", "grp"), None, None),
        P(("dom", "grp"), None),
        P(("dom", "grp"), None),
    )
    out_specs = (P(("dom", "grp"), None), P())
    return jax.shard_map(shards, mesh=mesh, in_specs=in_specs, out_specs=out_specs, check_vma=False)
```

profile of v0, /device:TPU:1, one launch (start us, length us, event | category | flops | bytes accessed | tf_op | source)
XLA Modules:
  0.0 366.0 jit_solution(14305169449429546651)
XLA Ops:
  10.2 1.2 copy.63
  13.7 23.4 %all_to_all.14 = f32[512,4,128]{2,1,0:T(4,128)S(1)} all-to-all(f32[512,4,128]{2,1,0:T(4,128)S(1)} %copy.64), channel_id=1, replica_groups=mesh['dom'=16,'grp'=16] {'grp'}, dimensions={0} | all-to-all | bytes 2097152 | tf_op jit(solution)/shard_map/all_to_all | solution.py:111
  37.5 1.4 fusion.15
  39.4 1.6 fusion.9
  42.0 14.1 %all-gather = s32[16,1,16]{2,1,0:T(1,128)S(1)} all-gather(s32[1,1,16]{2,1,0:T(1,128)S(1)} %bitcast.158), channel_id=1, replica_groups=mesh['dom'=16,'grp'=16] {'grp'}, dimensions={0}, use_global_device_ids=true | all-gather | bytes 1088 | tf_op jit(solution)/shard_map/all_gather | solution.py:118
  56.6 17.3 %all_gather.10 = s32[16,16,16]{2,1,0:T(8,128)S(1)} all-gather(s32[1,16,16]{2,1,0:T(8,128)S(1)} %copy-done.7), channel_id=1, replica_groups=mesh['dom'=16,'grp'=16] {'grp'}, dimensions={0}, use_global_device_ids=true | all-gather | bytes 17408 | tf_op jit(solution)/shard_map/all_gather | solution.py:117
  73.9 89.0 %all-reduce = (f32[3,1024]{1,0:T(4,128)S(1)}, f32[1024]{0:T(1024)S(1)}) all-reduce(f32[3,1024]{1,0:T(4,128)S(1)} %slice.60, f32[1024]{0:T(1024)S(1)} %bitcast.154), channel_id=1, replica_groups=mesh['dom'=16,'grp'=16] {'dom','grp'}, use_global_device_ids=true, to_apply=%region_0.1 | all-reduce | flops 4096 | bytes 32768 | tf_op jit(solution)/shard_map/psum | solution.py:89
  163.1 1.1 fusion.13
  165.0 1.9 copy.66
  166.9 1.3 fusion.10
  168.6 1.5 pad_maximum_fusion
  170.1 1.7 copy.70
  171.8 104.0 %while.12 = (s32[]{:T(128)}, f32[16,32,128]{2,1,0:T(8,128)S(1)}, s32[16,32,4]{1,0,2:T(8,128)}, f32[768,4,128]{0,2,1:T(8,128)S(1)}, f32[16,32,4,128]{3,2,1,0:T(4,128)S(1)}, /*index=5*/s32[]{:T(128)}) while((s32[]{:T(128)}, f32[16,32,128]{2,1,0:T(8,128)S(1)}, s32[16,32,4]{1,0,2:T(8,128)}, f32[768,4,128]{0,2,1:T(8,128)S(1)}, ...), condition=%wide.region_8.9_spmd, body=%wide.region_6.8_spmd.sunk | while | flops 627146752 | bytes 3606097 | solution.py:41
  172.7 1.0 fusion.63
  174.0 4.4 %multiply_reduce_fusion.2 = f32[32,128]{1,0:T(8,128)S(1)} fusion(f32[32,4,128]{2,1,0:T(4,128)S(1)} %copy.88, f32[32,128]{1,0:T(8,128)S(1)} %get-tuple-element.135, f32[32,4,128]{2,1,0:T(4,128)S(1)} %copy.90, f32[32,128]{1,0:T(8,128)S(1)} %get-tuple-element.137, f32[32,4,128]{2,1,0:T(4,128)S(1)} %copy.91, f32[32,128]{1,0:T(8,128)S(1)} %get-tuple-element.139, ...), kind=kLoop, calls=%fused_computation.clone.1 | loop fusion | flops 23064576 | bytes 327680 | tf_op jit(solution)/shard_map/while/body/eval_jaxpr/reduce_sum | solution.py:28
  179.1 1.0 fusion.63
  180.5 4.4 %multiply_reduce_fusion.2 = f32[32,128]{1,0:T(8,128)S(1)} fusion(f32[32,4,128]{2,1,0:T(4,128)S(1)} %copy.88, f32[32,128]{1,0:T(8,128)S(1)} %get-tuple-element.135, f32[32,4,128]{2,1,0:T(4,128)S(1)} %copy.90, f32[32,128]{1,0:T(8,128)S(1)} %get-tuple-element.137, f32[32,4,128]{2,1,0:T(4,128)S(1)} %copy.91, f32[32,128]{1,0:T(8,128)S(1)} %get-tuple-element.139, ...), kind=kLoop, calls=%fused_computation.clone.1 | loop fusion | flops 23064576 | bytes 327680 | tf_op jit(solution)/shard_map/while/body/eval_jaxpr/reduce_sum | solution.py:28
  185.6 1.0 fusion.63
  187.0 4.4 %multiply_reduce_fusion.2 = f32[32,128]{1,0:T(8,128)S(1)} fusion(f32[32,4,128]{2,1,0:T(4,128)S(1)} %copy.88, f32[32,128]{1,0:T(8,128)S(1)} %get-tuple-element.135, f32[32,4,128]{2,1,0:T(4,128)S(1)} %copy.90, f32[32,128]{1,0:T(8,128)S(1)} %get-tuple-element.137, f32[32,4,128]{2,1,0:T(4,128)S(1)} %copy.91, f32[32,128]{1,0:T(8,128)S(1)} %get-tuple-element.139, ...), kind=kLoop, calls=%fused_computation.clone.1 | loop fusion | flops 23064576 | bytes 327680 | tf_op jit(solution)/shard_map/while/body/eval_jaxpr/reduce_sum | solution.py:28
  192.1 1.0 fusion.63
  193.5 4.4 %multiply_reduce_fusion.2 = f32[32,128]{1,0:T(8,128)S(1)} fusion(f32[32,4,128]{2,1,0:T(4,128)S(1)} %copy.88, f32[32,128]{1,0:T(8,128)S(1)} %get-tuple-element.135, f32[32,4,128]{2,1,0:T(4,128)S(1)} %copy.90, f32[32,128]{1,0:T(8,128)S(1)} %get-tuple-element.137, f32[32,4,128]{2,1,0:T(4,128)S(1)} %copy.91, f32[32,128]{1,0:T(8,128)S(1)} %get-tuple-element.139, ...), kind=kLoop, calls=%fused_computation.clone.1 | loop fusion | flops 23064576 | bytes 327680 | tf_op jit(solution)/shard_map/while/body/eval_jaxpr/reduce_sum | solution.py:28
  198.6 1.0 fusion.63
  200.0 4.4 %multiply_reduce_fusion.2 = f32[32,128]{1,0:T(8,128)S(1)} fusion(f32[32,4,128]{2,1,0:T(4,128)S(1)} %copy.88, f32[32,128]{1,0:T(8,128)S(1)} %get-tuple-element.135, f32[32,4,128]{2,1,0:T(4,128)S(1)} %copy.90, f32[32,128]{1,0:T(8,128)S(1)} %get-tuple-element.137, f32[32,4,128]{2,1,0:T(4,128)S(1)} %copy.91, f32[32,128]{1,0:T(8,128)S(1)} %get-tuple-element.139, ...), kind=kLoop, calls=%fused_computation.clone.1 | loop fusion | flops 23064576 | bytes 327680 | tf_op jit(solution)/shard_map/while/body/eval_jaxpr/reduce_sum | solution.py:28
  205.1 1.0 fusion.63
  206.5 4.4 %multiply_reduce_fusion.2 = f32[32,128]{1,0:T(8,128)S(1)} fusion(f32[32,4,128]{2,1,0:T(4,128)S(1)} %copy.88, f32[32,128]{1,0:T(8,128)S(1)} %get-tuple-element.135, f32[32,4,128]{2,1,0:T(4,128)S(1)} %copy.90, f32[32,128]{1,0:T(8,128)S(1)} %get-tuple-element.137, f32[32,4,128]{2,1,0:T(4,128)S(1)} %copy.91, f32[32,128]{1,0:T(8,128)S(1)} %get-tuple-element.139, ...), kind=kLoop, calls=%fused_computation.clone.1 | loop fusion | flops 23064576 | bytes 327680 | tf_op jit(solution)/shard_map/while/body/eval_jaxpr/reduce_sum | solution.py:28
  213.0 4.4 %multiply_reduce_fusion.2 = f32[32,128]{1,0:T(8,128)S(1)} fusion(f32[32,4,128]{2,1,0:T(4,128)S(1)} %copy.88, f32[32,128]{1,0:T(8,128)S(1)} %get-tuple-element.135, f32[32,4,128]{2,1,0:T(4,128)S(1)} %copy.90, f32[32,128]{1,0:T(8,128)S(1)} %get-tuple-element.137, f32[32,4,128]{2,1,0:T(4,128)S(1)} %copy.91, f32[32,128]{1,0:T(8,128)S(1)} %get-tuple-element.139, ...), kind=kLoop, calls=%fused_computation.clone.1 | loop fusion | flops 23064576 | bytes 327680 | tf_op jit(solution)/shard_map/while/body/eval_jaxpr/reduce_sum | solution.py:28
  218.1 1.0 fusion.63
  219.4 4.4 %multiply_reduce_fusion.2 = f32[32,128]{1,0:T(8,128)S(1)} fusion(f32[32,4,128]{2,1,0:T(4,128)S(1)} %copy.88, f32[32,128]{1,0:T(8,128)S(1)} %get-tuple-element.135, f32[32,4,128]{2,1,0:T(4,128)S(1)} %copy.90, f32[32,128]{1,0:T(8,128)S(1)} %get-tuple-element.137, f32[32,4,128]{2,1,0:T(4,128)S(1)} %copy.91, f32[32,128]{1,0:T(8,128)S(1)} %get-tuple-element.139, ...), kind=kLoop, calls=%fused_computation.clone.1 | loop fusion | flops 23064576 | bytes 327680 | tf_op jit(solution)/shard_map/while/body/eval_jaxpr/reduce_sum | solution.py:28
  224.6 1.0 fusion.63
  225.9 4.4 %multiply_reduce_fusion.2 = f32[32,128]{1,0:T(8,128)S(1)} fusion(f32[32,4,128]{2,1,0:T(4,128)S(1)} %copy.88, f32[32,128]{1,0:T(8,128)S(1)} %get-tuple-element.135, f32[32,4,128]{2,1,0:T(4,128)S(1)} %copy.90, f32[32,128]{1,0:T(8,128)S(1)} %get-tuple-element.137, f32[32,4,128]{2,1,0:T(4,128)S(1)} %copy.91, f32[32,128]{1,0:T(8,128)S(1)} %get-tuple-element.139, ...), kind=kLoop, calls=%fused_computation.clone.1 | loop fusion | flops 23064576 | bytes 327680 | tf_op jit(solution)/shard_map/while/body/eval_jaxpr/reduce_sum | solution.py:28
  231.1 1.0 fusion.63
  232.4 4.4 %multiply_reduce_fusion.2 = f32[32,128]{1,0:T(8,128)S(1)} fusion(f32[32,4,128]{2,1,0:T(4,128)S(1)} %copy.88, f32[32,128]{1,0:T(8,128)S(1)} %get-tuple-element.135, f32[32,4,128]{2,1,0:T(4,128)S(1)} %copy.90, f32[32,128]{1,0:T(8,128)S(1)} %get-tuple-element.137, f32[32,4,128]{2,1,0:T(4,128)S(1)} %copy.91, f32[32,128]{1,0:T(8,128)S(1)} %get-tuple-element.139, ...), kind=kLoop, calls=%fused_computation.clone.1 | loop fusion | flops 23064576 | bytes 327680 | tf_op jit(solution)/shard_map/while/body/eval_jaxpr/reduce_sum | solution.py:28
  237.6 1.0 fusion.63
  238.9 4.4 %multiply_reduce_fusion.2 = f32[32,128]{1,0:T(8,128)S(1)} fusion(f32[32,4,128]{2,1,0:T(4,128)S(1)} %copy.88, f32[32,128]{1,0:T(8,128)S(1)} %get-tuple-element.135, f32[32,4,128]{2,1,0:T(4,128)S(1)} %copy.90, f32[32,128]{1,0:T(8,128)S(1)} %get-tuple-element.137, f32[32,4,128]{2,1,0:T(4,128)S(1)} %copy.91, f32[32,128]{1,0:T(8,128)S(1)} %get-tuple-element.139, ...), kind=kLoop, calls=%fused_computation.clone.1 | loop fusion | flops 23064576 | bytes 327680 | tf_op jit(solution)/shard_map/while/body/eval_jaxpr/reduce_sum | solution.py:28
  244.1 1.0 fusion.63
  245.4 4.4 %multiply_reduce_fusion.2 = f32[32,128]{1,0:T(8,128)S(1)} fusion(f32[32,4,128]{2,1,0:T(4,128)S(1)} %copy.88, f32[32,128]{1,0:T(8,128)S(1)} %get-tuple-element.135, f32[32,4,128]{2,1,0:T(4,128)S(1)} %copy.90, f32[32,128]{1,0:T(8,128)S(1)} %get-tuple-element.137, f32[32,4,128]{2,1,0:T(4,128)S(1)} %copy.91, f32[32,128]{1,0:T(8,128)S(1)} %get-tuple-element.139, ...), kind=kLoop, calls=%fused_computation.clone.1 | loop fusion | flops 23064576 | bytes 327680 | tf_op jit(solution)/shard_map/while/body/eval_jaxpr/reduce_sum | solution.py:28
  250.6 1.0 fusion.63
  251.9 4.4 %multiply_reduce_fusion.2 = f32[32,128]{1,0:T(8,128)S(1)} fusion(f32[32,4,128]{2,1,0:T(4,128)S(1)} %copy.88, f32[32,128]{1,0:T(8,128)S(1)} %get-tuple-element.135, f32[32,4,128]{2,1,0:T(4,128)S(1)} %copy.90, f32[32,128]{1,0:T(8,128)S(1)} %get-tuple-element.137, f32[32,4,128]{2,1,0:T(4,128)S(1)} %copy.91, f32[32,128]{1,0:T(8,128)S(1)} %get-tuple-element.139, ...), kind=kLoop, calls=%fused_computation.clone.1 | loop fusion | flops 23064576 | bytes 327680 | tf_op jit(solution)/shard_map/while/body/eval_jaxpr/reduce_sum | solution.py:28
  257.1 1.0 fusion.63
  258.4 4.4 %multiply_reduce_fusion.2 = f32[32,128]{1,0:T(8,128)S(1)} fusion(f32[32,4,128]{2,1,0:T(4,128)S(1)} %copy.88, f32[32,128]{1,0:T(8,128)S(1)} %get-tuple-element.135, f32[32,4,128]{2,1,0:T(4,128)S(1)} %copy.90, f32[32,128]{1,0:T(8,128)S(1)} %get-tuple-element.137, f32[32,4,128]{2,1,0:T(4,128)S(1)} %copy.91, f32[32,128]{1,0:T(8,128)S(1)} %get-tuple-element.139, ...), kind=kLoop, calls=%fused_computation.clone.1 | loop fusion | flops 23064576 | bytes 327680 | tf_op jit(solution)/shard_map/while/body/eval_jaxpr/reduce_sum | solution.py:28
  263.6 1.0 fusion.63
  264.9 4.4 %multiply_reduce_fusion.2 = f32[32,128]{1,0:T(8,128)S(1)} fusion(f32[32,4,128]{2,1,0:T(4,128)S(1)} %copy.88, f32[32,128]{1,0:T(8,128)S(1)} %get-tuple-element.135, f32[32,4,128]{2,1,0:T(4,128)S(1)} %copy.90, f32[32,128]{1,0:T(8,128)S(1)} %get-tuple-element.137, f32[32,4,128]{2,1,0:T(4,128)S(1)} %copy.91, f32[32,128]{1,0:T(8,128)S(1)} %get-tuple-element.139, ...), kind=kLoop, calls=%fused_computation.clone.1 | loop fusion | flops 23064576 | bytes 327680 | tf_op jit(solution)/shard_map/while/body/eval_jaxpr/reduce_sum | solution.py:28
  270.0 1.0 fusion.63
  271.4 4.4 %multiply_reduce_fusion.2 = f32[32,128]{1,0:T(8,128)S(1)} fusion(f32[32,4,128]{2,1,0:T(4,128)S(1)} %copy.88, f32[32,128]{1,0:T(8,128)S(1)} %get-tuple-element.135, f32[32,4,128]{2,1,0:T(4,128)S(1)} %copy.90, f32[32,128]{1,0:T(8,128)S(1)} %get-tuple-element.137, f32[32,4,128]{2,1,0:T(4,128)S(1)} %copy.91, f32[32,128]{1,0:T(8,128)S(1)} %get-tuple-element.139, ...), kind=kLoop, calls=%fused_computation.clone.1 | loop fusion | flops 23064576 | bytes 327680 | tf_op jit(solution)/shard_map/while/body/eval_jaxpr/reduce_sum | solution.py:28
  276.5 3.5 all-to-all-start.1
  280.1 1.4 fusion.14
  281.7 75.6 %psum.23 = f32[1024]{0:T(1024)S(1)} all-reduce(f32[1024]{0:T(1024)S(1)} %bitcast.156), channel_id=1, replica_groups=mesh['dom'=16,'grp'=16] {'dom','grp'}, use_global_device_ids=true, to_apply=%region_9.10 | all-reduce | flops 1024 | bytes 8192 | tf_op jit(solution)/shard_map/psum | solution.py:97
  357.9 1.3 convolution_add_fusion
  (224 shorter events, 27.0 us)
Async XLA Ops:
  7.2 157.8 %all-gather.3.cloned.1.call-start = ((), (), s32[]{:S(2)}) async-start(), calls=%async_computation.2 | async-start | bytes 2228224 | tf_op jit(solution)/shard_map/all_gather | solution.py:115
  13.7 23.8 %copy-start.10 = (s32[1,64]{1,0:T(1,128)S(1)}, s32[1,64]{1,0:T(1,128)}, u32[]{:S(2)}) copy-start(s32[1,64]{1,0:T(1,128)} %param.16) | copy-start | bytes 772
  37.1 1.8 copy-start
  37.1 1.8 copy-start.1
  37.1 2.2 copy-start.3
  37.5 3.8 %copy-start.6 = (s32[512,4]{0,1:T(4,128)S(1)}, s32[512,4]{0,1:T(4,128)}, u32[]{:S(2)}) copy-start(s32[512,4]{0,1:T(4,128)} %param.19) | copy-start | bytes 24580
  37.5 4.5 %copy-start.11 = (s32[1,16]{1,0:T(1,128)S(1)}, s32[1,16]{1,0:T(1,128)}, u32[]{:S(2)}) copy-start(s32[1,16]{1,0:T(1,128)} %param.18) | copy-start | bytes 196
  37.5 19.0 %copy-start.7 = (s32[1,16,16]{2,1,0:T(8,128)S(1)}, s32[1,16,16]{2,1,0:T(8,128)}, u32[]{:S(2)}) copy-start(s32[1,16,16]{2,1,0:T(8,128)} %param.17) | copy-start | bytes 3076
  39.3 125.7 %copy-start.12 = (s32[16]{0:T(128)}, s32[16]{0:T(128)S(1)}, u32[]{:S(2)}) copy-start(s32[16]{0:T(128)S(1)} %and_select_fusion) | copy-start | bytes 196
  39.4 125.6 %copy-start.4 = (s32[32768]{0:T(1024)}, s32[32768]{0:T(1024)S(1)}, u32[]{:S(2)}) copy-start(s32[32768]{0:T(1024)S(1)} %add_select_fusion) | copy-start | bytes 393220
  162.8 1.4 copy-start.8
  171.8 108.3 %copy-start.2 = (f32[32768]{0:T(1024)S(1)}, f32[32768]{0:T(1024)}, u32[]{:S(2)}) copy-start(f32[32768]{0:T(1024)} %multiply_multiply_fusion) | copy-start | bytes 393220
  171.8 108.3 %copy-start.5 = (s32[32768]{0:T(1024)S(1)}, s32[32768]{0:T(1024)}, u32[]{:S(2)}) copy-start(s32[32768]{0:T(1024)} %copy-done.4) | copy-start | bytes 393220
  171.8 109.7 %copy-start.13 = (s32[16]{0:T(128)S(1)}, s32[16]{0:T(128)}, u32[]{:S(2)}) copy-start(s32[16]{0:T(128)} %copy-done.12) | copy-start | bytes 196
  171.8 185.5 %copy-start.9 = (f32[1024]{0:T(1024)S(1)}, f32[1024]{0:T(1024)}, u32[]{:S(2)}) copy-start(f32[1024]{0:T(1024)} %copy-done.8) | copy-start | bytes 12292
  276.5 81.4 %all-to-all-start.1 = ((f32[16,32,128]{2,1,0:T(8,128)}), f32[16,32,128]{2,1,0:T(8,128)S(1)}, u32[]{:S(2)}, u32[]{:S(2)}) async-start(f32[16,32,128]{2,1,0:T(8,128)} %broadcast_multiply_fusion), calls=%async_computation.1 | async-start | bytes 524288 | tf_op jit(solution)/shard_map/all_to_all | solution.py:131
Sparse Core Ops, SparseCore 0:
  39.0 48.9 all-gather.2
where the time goes:
time: 367 us; the launch traced here: 366 us
  blocking collectives  219 us (60%)
  other arithmetic  77.5 us (21%)
  matrix products  26 us (7%)
  local copies, waits for them, and re-layouts  23.5 us (6%)
  between operations  14.4 us (4%)
    psum x1, blocking collectives, shards(): lax.psum((first_sums[0], first_sums[1:]), ('dom', 'grp'))  89 us
    psum x1, blocking collectives, shards(): lax.psum(group_sums((mass_flat * kinetic)[None, :])[0], ('dom', 'grp'))  75.6 us
    reduce_sum x16, other arithmetic, tile_potential(): return -jnp.sum(weights, axis=(1, 3))  70.1 us
    all_to_all x1, blocking collectives, shards(): lax.all_to_all(outgoing, 'grp', split_axis=0, concat_axis=0, tiled=True)  23.4 us
    dot_general x18, matrix products, select_rows(): jnp.dot(picker, flat, precision=exact, preferred_element_type=jnp.float32)  19.3 us
    all_gather x1, blocking collectives, shards(): lax.all_gather(send_list, 'grp', axis=0, tiled=True)  17.3 us
    all_gather x1, blocking collectives, shards(): lax.all_gather(send_count, 'grp', axis=0, tiled=True)  14.1 us
    dynamic_slice x48, local copies, waits for them, and re-layouts, slot_potential(): lax.map(one_block, (owned.reshape(slot_count // block_rows, block_rows, 4...  12.1 us
  transfers between devices with their start and end apart: 2, of which 0 were waited for; matrix products, arithmetic and copies ran while one was open for 2% of the time, Pallas kernels for 0%

commit v1 on v0

--- a/solution.py
+++ b/solution.py
@@ -1,3 +1,4 @@
+import functools
 import jax
 import jax.numpy as jnp
 from jax import lax
@@ -7,6 +8,22 @@
 GROUP_DEV = 4
 softening = 0.0025
 exact = lax.Precision.HIGHEST
+
+
+def match_bench(view, ax_name):
+    o_now = jnp.concatenate(
+        lax.all_to_all(
+            jnp.stack(tuple((view for _ in range(lax.axis_size(ax_name)))), axis=0),
+            axis_name=ax_name,
+            split_axis=0,
+            concat_axis=0,
+        ),
+        0,
+    )
+    return o_now
+
+
+_produce_task = functools.partial(match_bench, ax_name="grp")
 
 
 def select_rows(table, index):
@@ -115,7 +132,7 @@
     every_set = lax.all_gather(boundary, "grp", axis=0, tiled=True)
     all_lists, all_counts = (
         lax.all_gather(send_list, "grp", axis=0, tiled=True),
-        lax.all_gather(send_count, "grp", axis=0, tiled=True),
+        _produce_task(send_count),
     )
     my_index = lax.axis_index("grp")
     my_lists = jnp.take(all_lists, my_index, axis=1)

time: 367 us -> 355 us (0.967)
  blocking collectives: 219 us -> 203 us
    all_gather x1 -> x0, blocking collectives: 14.1 us -> none  [shards(): lax.all_gather(send_count, 'grp', axis=0, tiled=True)]
  transfers between devices with their start and end apart: 2 -> 3, of which waited for: 0 -> 0; matrix products, arithmetic and copies ran while one was open for 2% -> 3% of each run, Pallas kernels for 0% -> 0%
where the time goes in v1:
time: 355 us; the launch traced here: 354 us
  blocking collectives  203 us (57%)
  other arithmetic  77.5 us (22%)
  matrix products  26 us (7%)
  local copies, waits for them, and re-layouts  24.1 us (7%)
  between operations  14.4 us (4%)
  starting transfers between devices  7.06 us (2%)
    psum x1, blocking collectives, shards(): lax.psum((first_sums[0], first_sums[1:]), ('dom', 'grp'))  85.8 us
    psum x1, blocking collectives, shards(): lax.psum(group_sums((mass_flat * kinetic)[None, :])[0], ('dom', 'grp'))  75.6 us
    reduce_sum x16, other arithmetic, tile_potential(): return -jnp.sum(weights, axis=(1, 3))  70.1 us
    all_to_all x1, blocking collectives, shards(): lax.all_to_all(outgoing, 'grp', split_axis=0, concat_axis=0, tiled=True)  23.4 us
    dot_general x18, matrix products, select_rows(): jnp.dot(picker, flat, precision=exact, preferred_element_type=jnp.float32)  19.3 us
    all_gather x1, blocking collectives, shards(): lax.all_gather(send_list, 'grp', axis=0, tiled=True)  18.4 us
    dynamic_slice x48, local copies, waits for them, and re-layouts, slot_potential(): lax.map(one_block, (owned.reshape(slot_count // block_rows, block_rows, 4...  12.1 us
  transfers between devices with their start and end apart: 3, of which 0 were waited for; matrix products, arithmetic and copies ran while one was open for 3% of the time, Pallas kernels for 0%

profile of v1, /device:TPU:1, one launch (start us, length us, event | category | flops | bytes accessed | tf_op | source)
XLA Modules:
  0.0 354.0 jit_solution(12538834795533487769)
XLA Ops:
  10.1 1.2 copy.63
  13.6 23.4 %all_to_all.19 = f32[512,4,128]{2,1,0:T(4,128)S(1)} all-to-all(f32[512,4,128]{2,1,0:T(4,128)S(1)} %copy.64), channel_id=1, replica_groups=mesh['dom'=16,'grp'=16] {'grp'}, dimensions={0} | all-to-all | bytes 2097152 | tf_op jit(solution)/shard_map/all_to_all | solution.py:128
  37.7 3.5 all-to-all-start.1
  41.6 1.4 fusion.15
  43.5 1.6 fusion.9
  45.4 18.4 %all_gather.6 = s32[16,16,16]{2,1,0:T(8,128)S(1)} all-gather(s32[1,16,16]{2,1,0:T(8,128)S(1)} %copy-done.6), channel_id=1, replica_groups=mesh['dom'=16,'grp'=16] {'grp'}, dimensions={0}, use_global_device_ids=true | all-gather | bytes 17408 | tf_op jit(solution)/shard_map/all_gather | solution.py:134
  63.8 85.8 %all-reduce = (f32[3,1024]{1,0:T(4,128)S(1)}, f32[1024]{0:T(1024)S(1)}) all-reduce(f32[3,1024]{1,0:T(4,128)S(1)} %slice.60, f32[1024]{0:T(1024)S(1)} %bitcast.154), channel_id=1, replica_groups=mesh['dom'=16,'grp'=16] {'dom','grp'}, use_global_device_ids=true, to_apply=%region_0.1 | all-reduce | flops 4096 | bytes 32768 | tf_op jit(solution)/shard_map/psum | solution.py:106
  149.8 1.1 fusion.13
  153.0 1.9 copy.66
  154.9 1.3 fusion.10
  156.6 1.5 pad_maximum_fusion
  158.0 1.7 copy.70
  159.8 104.0 %while.12 = (s32[]{:T(128)}, f32[16,32,128]{2,1,0:T(8,128)S(1)}, s32[16,32,4]{1,0,2:T(8,128)}, f32[768,4,128]{0,2,1:T(8,128)S(1)}, f32[16,32,4,128]{3,2,1,0:T(4,128)S(1)}, /*index=5*/s32[]{:T(128)}) while((s32[]{:T(128)}, f32[16,32,128]{2,1,0:T(8,128)S(1)}, s32[16,32,4]{1,0,2:T(8,128)}, f32[768,4,128]{0,2,1:T(8,128)S(1)}, ...), condition=%wide.region_8.9_spmd, body=%wide.region_6.8_spmd.sunk | while | flops 627146752 | bytes 3606097 | solution.py:58
  160.6 1.0 fusion.63
  162.0 4.4 %multiply_reduce_fusion.2 = f32[32,128]{1,0:T(8,128)S(1)} fusion(f32[32,4,128]{2,1,0:T(4,128)S(1)} %copy.88, f32[32,128]{1,0:T(8,128)S(1)} %get-tuple-element.135, f32[32,4,128]{2,1,0:T(4,128)S(1)} %copy.90, f32[32,128]{1,0:T(8,128)S(1)} %get-tuple-element.137, f32[32,4,128]{2,1,0:T(4,128)S(1)} %copy.91, f32[32,128]{1,0:T(8,128)S(1)} %get-tuple-element.139, ...), kind=kLoop, calls=%fused_computation.clone.1 | loop fusion | flops 23064576 | bytes 327680 | tf_op jit(solution)/shard_map/while/body/eval_jaxpr/reduce_sum | solution.py:45
  167.1 1.0 fusion.63
  168.4 4.4 %multiply_reduce_fusion.2 = f32[32,128]{1,0:T(8,128)S(1)} fusion(f32[32,4,128]{2,1,0:T(4,128)S(1)} %copy.88, f32[32,128]{1,0:T(8,128)S(1)} %get-tuple-element.135, f32[32,4,128]{2,1,0:T(4,128)S(1)} %copy.90, f32[32,128]{1,0:T(8,128)S(1)} %get-tuple-element.137, f32[32,4,128]{2,1,0:T(4,128)S(1)} %copy.91, f32[32,128]{1,0:T(8,128)S(1)} %get-tuple-element.139, ...), kind=kLoop, calls=%fused_computation.clone.1 | loop fusion | flops 23064576 | bytes 327680 | tf_op jit(solution)/shard_map/while/body/eval_jaxpr/reduce_sum | solution.py:45
  173.6 1.0 fusion.63
  174.9 4.4 %multiply_reduce_fusion.2 = f32[32,128]{1,0:T(8,128)S(1)} fusion(f32[32,4,128]{2,1,0:T(4,128)S(1)} %copy.88, f32[32,128]{1,0:T(8,128)S(1)} %get-tuple-element.135, f32[32,4,128]{2,1,0:T(4,128)S(1)} %copy.90, f32[32,128]{1,0:T(8,128)S(1)} %get-tuple-element.137, f32[32,4,128]{2,1,0:T(4,128)S(1)} %copy.91, f32[32,128]{1,0:T(8,128)S(1)} %get-tuple-element.139, ...), kind=kLoop, calls=%fused_computation.clone.1 | loop fusion | flops 23064576 | bytes 327680 | tf_op jit(solution)/shard_map/while/body/eval_jaxpr/reduce_sum | solution.py:45
  180.1 1.0 fusion.63
  181.4 4.4 %multiply_reduce_fusion.2 = f32[32,128]{1,0:T(8,128)S(1)} fusion(f32[32,4,128]{2,1,0:T(4,128)S(1)} %copy.88, f32[32,128]{1,0:T(8,128)S(1)} %get-tuple-element.135, f32[32,4,128]{2,1,0:T(4,128)S(1)} %copy.90, f32[32,128]{1,0:T(8,128)S(1)} %get-tuple-element.137, f32[32,4,128]{2,1,0:T(4,128)S(1)} %copy.91, f32[32,128]{1,0:T(8,128)S(1)} %get-tuple-element.139, ...), kind=kLoop, calls=%fused_computation.clone.1 | loop fusion | flops 23064576 | bytes 327680 | tf_op jit(solution)/shard_map/while/body/eval_jaxpr/reduce_sum | solution.py:45
  186.6 1.0 fusion.63
  187.9 4.4 %multiply_reduce_fusion.2 = f32[32,128]{1,0:T(8,128)S(1)} fusion(f32[32,4,128]{2,1,0:T(4,128)S(1)} %copy.88, f32[32,128]{1,0:T(8,128)S(1)} %get-tuple-element.135, f32[32,4,128]{2,1,0:T(4,128)S(1)} %copy.90, f32[32,128]{1,0:T(8,128)S(1)} %get-tuple-element.137, f32[32,4,128]{2,1,0:T(4,128)S(1)} %copy.91, f32[32,128]{1,0:T(8,128)S(1)} %get-tuple-element.139, ...), kind=kLoop, calls=%fused_computation.clone.1 | loop fusion | flops 23064576 | bytes 327680 | tf_op jit(solution)/shard_map/while/body/eval_jaxpr/reduce_sum | solution.py:45
  193.1 1.0 fusion.63
  194.4 4.4 %multiply_reduce_fusion.2 = f32[32,128]{1,0:T(8,128)S(1)} fusion(f32[32,4,128]{2,1,0:T(4,128)S(1)} %copy.88, f32[32,128]{1,0:T(8,128)S(1)} %get-tuple-element.135, f32[32,4,128]{2,1,0:T(4,128)S(1)} %copy.90, f32[32,128]{1,0:T(8,128)S(1)} %get-tuple-element.137, f32[32,4,128]{2,1,0:T(4,128)S(1)} %copy.91, f32[32,128]{1,0:T(8,128)S(1)} %get-tuple-element.139, ...), kind=kLoop, calls=%fused_computation.clone.1 | loop fusion | flops 23064576 | bytes 327680 | tf_op jit(solution)/shard_map/while/body/eval_jaxpr/reduce_sum | solution.py:45
  199.6 1.0 fusion.63
  200.9 4.4 %multiply_reduce_fusion.2 = f32[32,128]{1,0:T(8,128)S(1)} fusion(f32[32,4,128]{2,1,0:T(4,128)S(1)} %copy.88, f32[32,128]{1,0:T(8,128)S(1)} %get-tuple-element.135, f32[32,4,128]{2,1,0:T(4,128)S(1)} %copy.90, f32[32,128]{1,0:T(8,128)S(1)} %get-tuple-element.137, f32[32,4,128]{2,1,0:T(4,128)S(1)} %copy.91, f32[32,128]{1,0:T(8,128)S(1)} %get-tuple-element.139, ...), kind=kLoop, calls=%fused_computation.clone.1 | loop fusion | flops 23064576 | bytes 327680 | tf_op jit(solution)/shard_map/while/body/eval_jaxpr/reduce_sum | solution.py:45
  206.1 1.0 fusion.63
  207.4 4.4 %multiply_reduce_fusion.2 = f32[32,128]{1,0:T(8,128)S(1)} fusion(f32[32,4,128]{2,1,0:T(4,128)S(1)} %copy.88, f32[32,128]{1,0:T(8,128)S(1)} %get-tuple-element.135, f32[32,4,128]{2,1,0:T(4,128)S(1)} %copy.90, f32[32,128]{1,0:T(8,128)S(1)} %get-tuple-element.137, f32[32,4,128]{2,1,0:T(4,128)S(1)} %copy.91, f32[32,128]{1,0:T(8,128)S(1)} %get-tuple-element.139, ...), kind=kLoop, calls=%fused_computation.clone.1 | loop fusion | flops 23064576 | bytes 327680 | tf_op jit(solution)/shard_map/while/body/eval_jaxpr/reduce_sum | solution.py:45
  212.6 1.0 fusion.63
  213.9 4.4 %multiply_reduce_fusion.2 = f32[32,128]{1,0:T(8,128)S(1)} fusion(f32[32,4,128]{2,1,0:T(4,128)S(1)} %copy.88, f32[32,128]{1,0:T(8,128)S(1)} %get-tuple-element.135, f32[32,4,128]{2,1,0:T(4,128)S(1)} %copy.90, f32[32,128]{1,0:T(8,128)S(1)} %get-tuple-element.137, f32[32,4,128]{2,1,0:T(4,128)S(1)} %copy.91, f32[32,128]{1,0:T(8,128)S(1)} %get-tuple-element.139, ...), kind=kLoop, calls=%fused_computation.clone.1 | loop fusion | flops 23064576 | bytes 327680 | tf_op jit(solution)/shard_map/while/body/eval_jaxpr/reduce_sum | solution.py:45
  219.0 1.0 fusion.63
  220.4 4.4 %multiply_reduce_fusion.2 = f32[32,128]{1,0:T(8,128)S(1)} fusion(f32[32,4,128]{2,1,0:T(4,128)S(1)} %copy.88, f32[32,128]{1,0:T(8,128)S(1)} %get-tuple-element.135, f32[32,4,128]{2,1,0:T(4,128)S(1)} %copy.90, f32[32,128]{1,0:T(8,128)S(1)} %get-tuple-element.137, f32[32,4,128]{2,1,0:T(4,128)S(1)} %copy.91, f32[32,128]{1,0:T(8,128)S(1)} %get-tuple-element.139, ...), kind=kLoop, calls=%fused_computation.clone.1 | loop fusion | flops 23064576 | bytes 327680 | tf_op jit(solution)/shard_map/while/body/eval_jaxpr/reduce_sum | solution.py:45
  226.9 4.4 %multiply_reduce_fusion.2 = f32[32,128]{1,0:T(8,128)S(1)} fusion(f32[32,4,128]{2,1,0:T(4,128)S(1)} %copy.88, f32[32,128]{1,0:T(8,128)S(1)} %get-tuple-element.135, f32[32,4,128]{2,1,0:T(4,128)S(1)} %copy.90, f32[32,128]{1,0:T(8,128)S(1)} %get-tuple-element.137, f32[32,4,128]{2,1,0:T(4,128)S(1)} %copy.91, f32[32,128]{1,0:T(8,128)S(1)} %get-tuple-element.139, ...), kind=kLoop, calls=%fused_computation.clone.1 | loop fusion | flops 23064576 | bytes 327680 | tf_op jit(solution)/shard_map/while/body/eval_jaxpr/reduce_sum | solution.py:45
  232.0 1.0 fusion.63
  233.4 4.4 %multiply_reduce_fusion.2 = f32[32,128]{1,0:T(8,128)S(1)} fusion(f32[32,4,128]{2,1,0:T(4,128)S(1)} %copy.88, f32[32,128]{1,0:T(8,128)S(1)} %get-tuple-element.135, f32[32,4,128]{2,1,0:T(4,128)S(1)} %copy.90, f32[32,128]{1,0:T(8,128)S(1)} %get-tuple-element.137, f32[32,4,128]{2,1,0:T(4,128)S(1)} %copy.91, f32[32,128]{1,0:T(8,128)S(1)} %get-tuple-element.139, ...), kind=kLoop, calls=%fused_computation.clone.1 | loop fusion | flops 23064576 | bytes 327680 | tf_op jit(solution)/shard_map/while/body/eval_jaxpr/reduce_sum | solution.py:45
  238.5 1.0 fusion.63
  239.9 4.4 %multiply_reduce_fusion.2 = f32[32,128]{1,0:T(8,128)S(1)} fusion(f32[32,4,128]{2,1,0:T(4,128)S(1)} %copy.88, f32[32,128]{1,0:T(8,128)S(1)} %get-tuple-element.135, f32[32,4,128]{2,1,0:T(4,128)S(1)} %copy.90, f32[32,128]{1,0:T(8,128)S(1)} %get-tuple-element.137, f32[32,4,128]{2,1,0:T(4,128)S(1)} %copy.91, f32[32,128]{1,0:T(8,128)S(1)} %get-tuple-element.139, ...), kind=kLoop, calls=%fused_computation.clone.1 | loop fusion | flops 23064576 | bytes 327680 | tf_op jit(solution)/shard_map/while/body/eval_jaxpr/reduce_sum | solution.py:45
  245.0 1.0 fusion.63
  246.4 4.4 %multiply_reduce_fusion.2 = f32[32,128]{1,0:T(8,128)S(1)} fusion(f32[32,4,128]{2,1,0:T(4,128)S(1)} %copy.88, f32[32,128]{1,0:T(8,128)S(1)} %get-tuple-element.135, f32[32,4,128]{2,1,0:T(4,128)S(1)} %copy.90, f32[32,128]{1,0:T(8,128)S(1)} %get-tuple-element.137, f32[32,4,128]{2,1,0:T(4,128)S(1)} %copy.91, f32[32,128]{1,0:T(8,128)S(1)} %get-tuple-element.139, ...), kind=kLoop, calls=%fused_computation.clone.1 | loop fusion | flops 23064576 | bytes 327680 | tf_op jit(solution)/shard_map/while/body/eval_jaxpr/reduce_sum | solution.py:45
  251.5 1.0 fusion.63
  252.9 4.4 %multiply_reduce_fusion.2 = f32[32,128]{1,0:T(8,128)S(1)} fusion(f32[32,4,128]{2,1,0:T(4,128)S(1)} %copy.88, f32[32,128]{1,0:T(8,128)S(1)} %get-tuple-element.135, f32[32,4,128]{2,1,0:T(4,128)S(1)} %copy.90, f32[32,128]{1,0:T(8,128)S(1)} %get-tuple-element.137, f32[32,4,128]{2,1,0:T(4,128)S(1)} %copy.91, f32[32,128]{1,0:T(8,128)S(1)} %get-tuple-element.139, ...), kind=kLoop, calls=%fused_computation.clone.1 | loop fusion | flops 23064576 | bytes 327680 | tf_op jit(solution)/shard_map/while/body/eval_jaxpr/reduce_sum | solution.py:45
  258.0 1.0 fusion.63
  259.3 4.4 %multiply_reduce_fusion.2 = f32[32,128]{1,0:T(8,128)S(1)} fusion(f32[32,4,128]{2,1,0:T(4,128)S(1)} %copy.88, f32[32,128]{1,0:T(8,128)S(1)} %get-tuple-element.135, f32[32,4,128]{2,1,0:T(4,128)S(1)} %copy.90, f32[32,128]{1,0:T(8,128)S(1)} %get-tuple-element.137, f32[32,4,128]{2,1,0:T(4,128)S(1)} %copy.91, f32[32,128]{1,0:T(8,128)S(1)} %get-tuple-element.139, ...), kind=kLoop, calls=%fused_computation.clone.1 | loop fusion | flops 23064576 | bytes 327680 | tf_op jit(solution)/shard_map/while/body/eval_jaxpr/reduce_sum | solution.py:45
  264.5 3.5 all-to-all-start.2
  268.0 1.4 fusion.14
  269.7 75.6 %psum.23 = f32[1024]{0:T(1024)S(1)} all-reduce(f32[1024]{0:T(1024)S(1)} %bitcast.156), channel_id=1, replica_groups=mesh['dom'=16,'grp'=16] {'dom','grp'}, use_global_device_ids=true, to_apply=%region_9.10 | all-reduce | flops 1024 | bytes 8192 | tf_op jit(solution)/shard_map/psum | solution.py:114
  345.9 1.3 convolution_add_fusion
  (226 shorter events, 27.6 us)
Async XLA Ops:
  12.9 24.1 %copy-start.11 = (s32[1,16]{1,0:T(1,128)S(1)}, s32[1,16]{1,0:T(1,128)}, u32[]{:S(2)}) copy-start(s32[1,16]{1,0:T(1,128)} %param.18) | copy-start | bytes 196
  13.6 28.0 %copy-start.10 = (s32[1,64]{1,0:T(1,128)S(1)}, s32[1,64]{1,0:T(1,128)}, u32[]{:S(2)}) copy-start(s32[1,64]{1,0:T(1,128)} %param.16) | copy-start | bytes 772
  37.1 5.9 %copy-start = (f32[256,128]{1,0:T(8,128)S(1)}, f32[256,128]{1,0:T(8,128)}, u32[]{:S(2)}) copy-start(f32[256,128]{1,0:T(8,128)} %param.13) | copy-start | bytes 393220
  37.1 6.0 %copy-start.1 = (f32[256,3,128]{2,0,1:T(8,128)S(1)}, f32[256,3,128]{2,0,1:T(8,128)}, u32[]{:S(2)}) copy-start(f32[256,3,128]{2,0,1:T(8,128)} %param.12) | copy-start | bytes 1179652
  37.7 114.7 %all-to-all-start.1 = ((s32[16,1,16]{2,1,0:T(1,128)}), s32[16,1,16]{2,1,0:T(1,128)S(1)}, u32[]{:S(2)}, u32[]{:S(2)}) async-start(s32[16,1,16]{2,1,0:T(1,128)} %stack.2), calls=%async_computation.1 | async-start | bytes 16384 | tf_op jit(solution)/shard_map/all_to_all | solution.py:15
  41.2 2.2 copy-start.3
  41.2 111.8 %all-gather.2.cloned.1.call-start = ((), (), s32[]{:S(2)}) async-start(), calls=%async_computation.3 | async-start | bytes 2228224 | tf_op jit(solution)/shard_map/all_gather | solution.py:132
  41.6 3.8 %copy-start.6 = (s32[1,16,16]{2,1,0:T(8,128)S(1)}, s32[1,16,16]{2,1,0:T(8,128)}, u32[]{:S(2)}) copy-start(s32[1,16,16]{2,1,0:T(8,128)} %param.17) | copy-start | bytes 3076
  43.4 108.3 %copy-start.7 = (s32[512,4]{0,1:T(4,128)S(1)}, s32[512,4]{0,1:T(4,128)}, u32[]{:S(2)}) copy-start(s32[512,4]{0,1:T(4,128)} %param.19) | copy-start | bytes 24580
  43.4 109.5 %copy-start.12 = (s32[16]{0:T(128)}, s32[16]{0:T(128)S(1)}, u32[]{:S(2)}) copy-start(s32[16]{0:T(128)S(1)} %and_select_fusion) | copy-start | bytes 196
  43.5 109.4 %copy-start.4 = (s32[32768]{0:T(1024)}, s32[32768]{0:T(1024)S(1)}, u32[]{:S(2)}) copy-start(s32[32768]{0:T(1024)S(1)} %add_select_fusion) | copy-start | bytes 393220
  149.6 3.3 copy-start.8
  159.7 108.3 %copy-start.2 = (f32[32768]{0:T(1024)S(1)}, f32[32768]{0:T(1024)}, u32[]{:S(2)}) copy-start(f32[32768]{0:T(1024)} %multiply_multiply_fusion) | copy-start | bytes 393220
  159.8 108.3 %copy-start.5 = (s32[32768]{0:T(1024)S(1)}, s32[32768]{0:T(1024)}, u32[]{:S(2)}) copy-start(s32[32768]{0:T(1024)} %copy-done.4) | copy-start | bytes 393220
  159.8 109.7 %copy-start.13 = (s32[16]{0:T(128)S(1)}, s32[16]{0:T(128)}, u32[]{:S(2)}) copy-start(s32[16]{0:T(128)} %copy-done.12) | copy-start | bytes 196
  159.8 185.5 %copy-start.9 = (f32[1024]{0:T(1024)S(1)}, f32[1024]{0:T(1024)}, u32[]{:S(2)}) copy-start(f32[1024]{0:T(1024)} %copy-done.8) | copy-start | bytes 12292
  264.5 81.4 %all-to-all-start.2 = ((f32[16,32,128]{2,1,0:T(8,128)}), f32[16,32,128]{2,1,0:T(8,128)S(1)}, u32[]{:S(2)}, u32[]{:S(2)}) async-start(f32[16,32,128]{2,1,0:T(8,128)} %broadcast_multiply_fusion), calls=%async_computation.2 | async-start | bytes 524288 | tf_op jit(solution)/shard_map/all_to_all | solution.py:148
Sparse Core Ops, SparseCore 0:
  45.0 53.1 all-gather.1
